TPU v7x, 32 devices: a whole 2x2x4 slice. The times are simulated.
32 devices in a mesh: parts: 2 (over y), tm: 4 (over x, core), cols: 4 (over z).
Axes of the slice: x: 2, y: 2, z: 4, core: 2. Of those that a mesh axis runs over, the one named last changes fastest.
Arguments:
- noise: float32 [16, 1024, 1024], P(('parts', 'tm'), None, 'cols'), parts along dimension 0, may hold values from -6 to 6
- inv_diag: float32 [16, 1024, 1024], P(('parts', 'tm'), None, 'cols'), parts along dimension 0, may hold values from -2 to 2, as said below
- coupling: float32 [16, 1024, 1024], P(('parts', 'tm'), None, 'cols'), parts along dimension 0, may hold values from -1 to 1, as said below
- order: int32 [1024], replicated, may hold values from 0 to 1023, each once
Outputs:
- sample: float32 [16, 1024, 1024], P(('parts', 'tm'), None, 'cols'), parts along dimension 0
There are 2 independent parts, one for each index of `parts`. A program takes and returns all parts, laid end to end along the dimension named above; an argument that names none is the same for every part. Nothing has to cross between parts.
Inputs may be any that keep to these rules, and one draw needn't show every extreme that they name: `order`: each of 0 to 1023 appears once. `inv_diag`: diagonal entries lie between 0.5 and 2, off-diagonal entries are small in magnitude. `coupling`: diagonal entries lie between 0.5 and 0.97, off-diagonal entries are small in magnitude.
All inputs are finite; a program needn't handle non-finite values.
Results may differ from a plain program's by a relative error of at most 0.00013.
Values sent between devices are 32-bit elements; how exact they have to be, the bound alone decides.
No kernel may reach another device: no remote copies, remote signals or barrier semaphores. Data moves between devices by JAX's collectives and lax.ppermute only.
A program may use at most 128 MiB of HBM per device.

v0:
```python
import jax
import jax.numpy as jnp
from jax import lax
from jax.sharding import PartitionSpec as P

precise = lax.Precision.HIGHEST


def shifted(block, axis, distance):
    devices = range(lax.axis_size(axis))
    route = [(i - distance, i) for i in devices if i - distance in devices]
    return lax.ppermute(block, axis, route)


def fold_with(operand, segment):
    return jnp.dot(segment, operand, precision=precise, preferred_element_type=jnp.float32)


def shards(noise, inv_diag, coupling, order):
    block_count = noise.shape[0]
    sample_count = noise.shape[2]
    driven = jnp.einsum(
        "kmn,kns->kms",
        lax.all_gather(inv_diag, "cols", axis=2, tiled=True),
        noise,
        precision=precise,
        preferred_element_type=jnp.float32,
    )
    local_field = driven[block_count - 1]
    reduced = coupling[block_count - 1]
    block = 0
    operand = jnp.concatenate([local_field, reduced], axis=1)
    product = fold_with(operand, lax.all_gather(coupling[block], "cols", axis=1, tiled=True))
    local_field = driven[block] + product[:, :sample_count]
    reduced = product[:, sample_count:]
    reduced_full = lax.all_gather(reduced, "cols", axis=1, tiled=True)

    def relay_step(step, carry):
        current, incoming = carry
        incoming = shifted(current, "tm", -1)
        current = local_field + jnp.dot(
            reduced_full, incoming, precision=precise, preferred_element_type=jnp.float32
        )
        return (current, incoming)

    _, entering = lax.fori_loop(
        0, lax.axis_size("tm"), relay_step, (local_field, jnp.zeros_like(local_field))
    )
    carried = entering
    results = [None] * block_count
    for block in range(block_count - 1, -1, -1):
        product = fold_with(carried, lax.all_gather(coupling[block], "cols", axis=1, tiled=True))
        carried = driven[block] + product
        results[block] = carried
    stacked = jnp.stack(results, axis=0)
    return jnp.take(stacked, order, axis=1)


def solution(mesh):
    return jax.shard_map(
        shards,
        mesh=mesh,
        in_specs=(
            P(("parts", "tm"), None, "cols"),
            P(("parts", "tm"), None, "cols"),
            P(("parts", "tm"), None, "cols"),
            P(),
        ),
        out_specs=P(("parts", "tm"), None, "cols"),
        check_vma=False,
    )
```

profile of v0, /device:TPU:1, one launch (start us, length us, event | category | flops | bytes accessed | tf_op | source)
XLA Modules:
  0.0 545.5 jit_solution(10568745071062961867)
XLA Ops:
  6.5 0.0 copy-start
  6.5 0.0 all-gather.7.cloned.1.call-start
  6.5 0.7 all-gather.7.cloned.1.call-update
  7.3 0.0 all-gather.11.cloned.1.call-start
  7.3 3.1 fusion.32
  10.4 0.0 all-gather.11.cloned.1.call-update
  10.4 0.0 all-gather.9.cloned.1.call-start
  10.4 1.6 copy.19
  12.0 0.0 copy-start.5
  12.0 148.9 %all-gather.7.cloned.1.call-done = f32[2,1024,1024]{2,1,0:T(8,128)} async-done(((f32[2,1024,256]{2,1,0:T(8,128)}), f32[2,1024,1024]{2,1,0:T(8,128)}) %all-gather.7.cloned.1.call-update) | async-done | bytes 8388624 | tf_op jit(solution)/shard_map/all_gather | solution.py:24
  160.9 0.0 copy-done
  160.9 9.8 %fusion.33 = f32[2,1024,256]{1,2,0:T(8,128)S(1)} fusion(f32[2,1024,1024]{2,1,0:T(8,128)} %all-gather.7.cloned.1.call-done, f32[2,1024,256]{2,1,0:T(8,128)S(1)} %copy-done), kind=kOutput, calls=%fused_computation.28 | convolution fusion | flops 6442450944 | bytes 12582912 | tf_op jit(solution)/shard_map/kmn,kns->kms/dot_general | solution.py:22
  170.7 0.0 copy-start.1
  170.7 1.3 copy-done.1
  172.0 1.1 slice_bitcast_fusion
  173.1 68.1 %all-gather.11.cloned.1.call-done = f32[1,1024,1024]{2,1,0:T(8,128)} async-done(((f32[1,1024,256]{2,1,0:T(8,128)}), f32[1,1024,1024]{2,1,0:T(8,128)}) %all-gather.11.cloned.1.call-update) | async-done | bytes 4194320 | tf_op jit(solution)/shard_map/all_gather | solution.py:52
  241.2 0.0 copy-done.5
  241.2 0.0 copy-start.2
  241.3 9.5 %fusion.9 = f32[1024,512]{0,1:T(8,128)S(1)} fusion(f32[1,1024,1024]{2,1,0:T(8,128)} %all-gather.11.cloned.1.call-done, f32[1024,256]{0,1:T(8,128)S(1)} %bitcast.59, f32[1024,256]{0,1:T(8,128)} %slice_bitcast_fusion), kind=kOutput, calls=%fused_computation.13 | convolution fusion | flops 6442975232 | bytes 8388608 | tf_op jit(solution)/shard_map/dot_general | solution.py:16
  250.7 0.0 copy-done.2
  250.7 1.6 fusion.31
  252.3 0.0 copy-start.6
  252.3 0.0 all-gather.9.cloned.1.call-update
  252.3 0.2 all-gather.13.cloned.1.call-start
  252.6 0.3 all-gather.13.cloned.1.call-update
  252.9 0.1 copy-done.6
  253.0 1.6 copy.13
  254.6 1.0 copy.21
  255.6 76.2 %all-gather.9.cloned.1.call-done = f32[1024,1024]{0,1:T(8,128)} async-done(((f32[1024,256]{0,1:T(8,128)}), f32[1024,1024]{0,1:T(8,128)}) %all-gather.9.cloned.1.call-update) | async-done | bytes 4194320 | tf_op jit(solution)/shard_map/all_gather | solution.py:36
  331.8 5.4 copy.14
  337.2 75.3 %all-gather.13.cloned.1.call-done = f32[1,1024,1024]{1,2,0:T(8,128)} async-done(((f32[1,1024,256]{1,2,0:T(8,128)}), f32[1,1024,1024]{1,2,0:T(8,128)}) %all-gather.13.cloned.1.call-update) | async-done | bytes 4194320 | tf_op jit(solution)/shard_map/all_gather | solution.py:52
  412.5 93.3 %while.12 = (s32[]{:T(128)}, f32[1024,256]{1,0:T(8,128)}, f32[1024,256]{1,0:T(8,128)}, f32[1024,1024]{1,0:T(8,128)}, f32[1024,256]{1,0:T(8,128)S(1)}, /*index=5*/s32[]{:T(128)}) while((s32[]{:T(128)}, f32[1024,256]{1,0:T(8,128)}, f32[1024,256]{1,0:T(8,128)}, f32[1024,1024]{1,0:T(8,128)}, f32[1024,256]{1,0:T(8,128)S(1)}, ...), condition=%wide.region_1.0_spmd, body=%wide.region_0.0_spmd.sunk | while | flops 3221487616 | bytes 11534445 | solution.py:46
  412.5 2.6 collective-permute-start
  415.1 13.9 %collective-permute-done = f32[1024,256]{1,0:T(8,128)} collective-permute-done((f32[1024,256]{1,0:T(8,128)}, f32[1024,256]{1,0:T(8,128)}, u32[]{:S(2)}, u32[]{:S(2)}) %collective-permute-start) | collective-permute-done | bytes 1048608 | tf_op jit(solution)/shard_map/while/body/eval_jaxpr/ppermute | solution.py:12
  429.0 6.9 %convolution_add_fusion.2 = f32[1024,256]{1,0:T(8,128)} fusion(f32[1024,256]{1,0:T(8,128)S(1)} %get-tuple-element.101, f32[1024,1024]{1,0:T(8,128)} %get-tuple-element.100, f32[1024,256]{1,0:T(8,128)} %collective-permute-done), kind=kOutput, calls=%fused_computation.1.clone.1 | convolution fusion | flops 3221487616 | bytes 7340032 | tf_op jit(solution)/shard_map/while/body/eval_jaxpr/dot_general | solution.py:41
  435.9 1.9 collective-permute-start
  437.8 14.5 %collective-permute-done = f32[1024,256]{1,0:T(8,128)} collective-permute-done((f32[1024,256]{1,0:T(8,128)}, f32[1024,256]{1,0:T(8,128)}, u32[]{:S(2)}, u32[]{:S(2)}) %collective-permute-start) | collective-permute-done | bytes 1048608 | tf_op jit(solution)/shard_map/while/body/eval_jaxpr/ppermute | solution.py:12
  452.3 6.9 %convolution_add_fusion.2 = f32[1024,256]{1,0:T(8,128)} fusion(f32[1024,256]{1,0:T(8,128)S(1)} %get-tuple-element.101, f32[1024,1024]{1,0:T(8,128)} %get-tuple-element.100, f32[1024,256]{1,0:T(8,128)} %collective-permute-done), kind=kOutput, calls=%fused_computation.1.clone.1 | convolution fusion | flops 3221487616 | bytes 7340032 | tf_op jit(solution)/shard_map/while/body/eval_jaxpr/dot_general | solution.py:41
  459.2 1.9 collective-permute-start
  461.1 14.5 %collective-permute-done = f32[1024,256]{1,0:T(8,128)} collective-permute-done((f32[1024,256]{1,0:T(8,128)}, f32[1024,256]{1,0:T(8,128)}, u32[]{:S(2)}, u32[]{:S(2)}) %collective-permute-start) | collective-permute-done | bytes 1048608 | tf_op jit(solution)/shard_map/while/body/eval_jaxpr/ppermute | solution.py:12
  475.6 6.9 %convolution_add_fusion.2 = f32[1024,256]{1,0:T(8,128)} fusion(f32[1024,256]{1,0:T(8,128)S(1)} %get-tuple-element.101, f32[1024,1024]{1,0:T(8,128)} %get-tuple-element.100, f32[1024,256]{1,0:T(8,128)} %collective-permute-done), kind=kOutput, calls=%fused_computation.1.clone.1 | convolution fusion | flops 3221487616 | bytes 7340032 | tf_op jit(solution)/shard_map/while/body/eval_jaxpr/dot_general | solution.py:41
  482.5 1.9 collective-permute-start
  484.5 14.5 %collective-permute-done = f32[1024,256]{1,0:T(8,128)} collective-permute-done((f32[1024,256]{1,0:T(8,128)}, f32[1024,256]{1,0:T(8,128)}, u32[]{:S(2)}, u32[]{:S(2)}) %collective-permute-start) | collective-permute-done | bytes 1048608 | tf_op jit(solution)/shard_map/while/body/eval_jaxpr/ppermute | solution.py:12
  499.0 6.9 %convolution_add_fusion.2 = f32[1024,256]{1,0:T(8,128)} fusion(f32[1024,256]{1,0:T(8,128)S(1)} %get-tuple-element.101, f32[1024,1024]{1,0:T(8,128)} %get-tuple-element.100, f32[1024,256]{1,0:T(8,128)} %collective-permute-done), kind=kOutput, calls=%fused_computation.1.clone.1 | convolution fusion | flops 3221487616 | bytes 7340032 | tf_op jit(solution)/shard_map/while/body/eval_jaxpr/dot_general | solution.py:41
  505.9 0.0 copy-start.3
  505.9 0.0 copy-start.4
  505.9 6.6 %fusion.26 = f32[1024,256]{0,1:T(8,128)S(1)} fusion(f32[1024,256]{1,0:T(8,128)} %get-tuple-element.31, f32[1,1024,1024]{1,2,0:T(8,128)} %all-gather.13.cloned.1.call-done, f32[2,1024,256]{1,2,0:T(8,128)} %copy-done.1), kind=kOutput, calls=%fused_computation.18 | convolution fusion | flops 3221487616 | bytes 7340032 | tf_op jit(solution)/shard_map/dot_general | solution.py:16
  512.4 0.0 copy-done.3
  512.4 0.0 copy-done.4
  512.4 3.7 fusion.20
  516.2 1.5 pad_maximum_fusion
  517.7 4.1 copy.16
  521.8 10.5 %gather_fusion = f32[1024,2,256]{2,1,0:T(2,128)} fusion(f32[2,1024,256]{2,0,1:T(2,128)} %copy.16, s32[1024]{0:T(1024)S(1)} %fusion.29), kind=kCustom, calls=%fused_computation | custom fusion | bytes 4198400 | tf_op jit(solution)/shard_map/jit(_take)/gather | solution.py:56
  532.3 5.2 select_bitcast_fusion
  537.5 1.5 copy.17
  (3 shorter events, 0.0 us)
Async XLA Ops:
  6.5 154.4 %copy-start = (f32[2,1024,256]{2,1,0:T(8,128)S(1)}, f32[2,1024,256]{2,1,0:T(8,128)}, u32[]{:S(2)}) copy-start(f32[2,1024,256]{2,1,0:T(8,128)} %param.6) | copy-start | bytes 6291460
  6.5 154.4 %all-gather.7.cloned.1.call-start = ((), (), s32[]{:S(2)}) async-start(), calls=%async_computation | async-start | bytes 10485760 | tf_op jit(solution)/shard_map/all_gather | solution.py:24
  7.3 234.0 %all-gather.11.cloned.1.call-start = ((), (), s32[]{:S(2)}) async-start(), calls=%async_computation.2 | async-start | bytes 5242880 | tf_op jit(solution)/shard_map/all_gather | solution.py:52
  10.4 321.4 %all-gather.9.cloned.1.call-start = ((), (), s32[]{:S(2)}) async-start(), calls=%async_computation.1 | async-start | bytes 5242880 | tf_op jit(solution)/shard_map/all_gather | solution.py:36
  12.0 229.2 %copy-start.5 = (f32[1,1024,256]{1,2,0:T(8,128)}, f32[1,1024,256]{1,2,0:T(8,128)S(1)}, u32[]{:S(2)}) copy-start(f32[1,1024,256]{1,2,0:T(8,128)S(1)} %copy.19) | copy-start | bytes 3145732
  170.7 1.3 copy-start.1
  241.2 9.5 %copy-start.2 = (f32[2,1024,256]{1,2,0:T(8,128)S(1)}, f32[2,1024,256]{1,2,0:T(8,128)}, u32[]{:S(2)}) copy-start(f32[2,1024,256]{1,2,0:T(8,128)} %copy-done.1) | copy-start | bytes 6291460
  252.3 0.7 copy-start.6
  252.3 160.2 %all-gather.13.cloned.1.call-start = ((), (), s32[]{:S(2)}) async-start(), calls=%async_computation.3 | async-start | bytes 5242880 | tf_op jit(solution)/shard_map/all_gather | solution.py:52
  412.5 16.5 %collective-permute-start = (f32[1024,256]{1,0:T(8,128)}, f32[1024,256]{1,0:T(8,128)}, u32[]{:S(2)}, u32[]{:S(2)}) collective-permute-start(f32[1024,256]{1,0:T(8,128)} %get-tuple-element.92), channel_id=1, source_target_pairs={{4,0},{8,4},{12,8},{5,1},{9,5},{13,9},{6,2},{10,6},{14,10},{7,3},{... | collective-permute-start | bytes 3145736 | tf_op jit(solution)/shard_map/while/body/eval_jaxpr/ppermute | solution.py:12
  435.9 16.4 %collective-permute-start = (f32[1024,256]{1,0:T(8,128)}, f32[1024,256]{1,0:T(8,128)}, u32[]{:S(2)}, u32[]{:S(2)}) collective-permute-start(f32[1024,256]{1,0:T(8,128)} %get-tuple-element.92), channel_id=1, source_target_pairs={{4,0},{8,4},{12,8},{5,1},{9,5},{13,9},{6,2},{10,6},{14,10},{7,3},{... | collective-permute-start | bytes 3145736 | tf_op jit(solution)/shard_map/while/body/eval_jaxpr/ppermute | solution.py:12
  459.2 16.4 %collective-permute-start = (f32[1024,256]{1,0:T(8,128)}, f32[1024,256]{1,0:T(8,128)}, u32[]{:S(2)}, u32[]{:S(2)}) collective-permute-start(f32[1024,256]{1,0:T(8,128)} %get-tuple-element.92), channel_id=1, source_target_pairs={{4,0},{8,4},{12,8},{5,1},{9,5},{13,9},{6,2},{10,6},{14,10},{7,3},{... | collective-permute-start | bytes 3145736 | tf_op jit(solution)/shard_map/while/body/eval_jaxpr/ppermute | solution.py:12
  482.5 16.4 %collective-permute-start = (f32[1024,256]{1,0:T(8,128)}, f32[1024,256]{1,0:T(8,128)}, u32[]{:S(2)}, u32[]{:S(2)}) collective-permute-start(f32[1024,256]{1,0:T(8,128)} %get-tuple-element.92), channel_id=1, source_target_pairs={{4,0},{8,4},{12,8},{5,1},{9,5},{13,9},{6,2},{10,6},{14,10},{7,3},{... | collective-permute-start | bytes 3145736 | tf_op jit(solution)/shard_map/while/body/eval_jaxpr/ppermute | solution.py:12
  505.9 6.6 %copy-start.3 = (f32[2,1024,256]{1,2,0:T(8,128)S(1)}, f32[2,1024,256]{1,2,0:T(8,128)}, u32[]{:S(2)}) copy-start(f32[2,1024,256]{1,2,0:T(8,128)} %copy-done.1) | copy-start | bytes 6291460
  505.9 6.6 %copy-start.4 = (f32[1,1024,1024]{2,1,0:T(8,128)S(1)}, f32[1,1024,1024]{2,1,0:T(8,128)}, u32[]{:S(2)}) copy-start(f32[1,1024,1024]{2,1,0:T(8,128)} %all-gather.11.cloned.1.call-done) | copy-start | bytes 12582916
Sparse Core Ops, SparseCore 0:
  8.9 151.9 all-gather.6
  162.5 78.7 all-gather.10
  252.5 79.2 all-gather.8
  333.2 79.2 all-gather.12
where the time goes:
time: 546 us
  waiting for transfers between devices  427 us (78%)
  matrix products  57.1 us (10%)
  local copies, waits for them, and re-layouts  31.2 us (6%)
  between operations  13.2 us (2%)
  starting transfers between devices  8.59 us (2%)
  other arithmetic  8.28 us (2%)
    all_gather x1, waiting for transfers between devices, shards(): lax.all_gather(inv_diag, 'cols', axis=2, tiled=True)  149 us
    all_gather x2, waiting for transfers between devices, shards(): lax.all_gather(coupling[block], 'cols', axis=1, tiled=True)  143 us
    all_gather x1, waiting for transfers between devices, shards(): reduced_full = lax.all_gather(reduced, 'cols', axis=1, tiled=True)  76.2 us
    ppermute x4, waiting for transfers between devices, shifted(): return lax.ppermute(block, axis, route)  57.4 us
    dot_general x4, matrix products, relay_step(): jnp.dot(reduced_full, incoming, precision=precise, preferred_element_type...  27.6 us
    dot_general x3, matrix products, fold_with(): jnp.dot(segment, operand, precision=precise, preferred_element_type=jnp.f...  19.8 us
  transfers between devices with their start and end apart: 8, of which 8 were waited for; matrix products, arithmetic and copies ran while one was open for 4% of the time, Pallas kernels for 0%

commit v1 on v0

--- a/solution.py
+++ b/solution.py
@@ -4,6 +4,18 @@
 from jax.sharding import PartitionSpec as P
 
 precise = lax.Precision.HIGHEST
+
+
+def summed_around(x, axis, dim, term):
+    length, place = (lax.axis_size(axis), lax.axis_index(axis))
+    behind = [(i, (i - 1) % length) for i in range(length)]
+    rows = x.shape[dim]
+    carried = x
+    total = term(carried, place * rows)
+    for hop in range(1, length):
+        carried = lax.ppermute(carried, axis, behind)
+        total = total + term(carried, (place + hop) % length * rows)
+    return total
 
 
 def shifted(block, axis, distance):
@@ -19,12 +31,17 @@
 def shards(noise, inv_diag, coupling, order):
     block_count = noise.shape[0]
     sample_count = noise.shape[2]
-    driven = jnp.einsum(
-        "kmn,kns->kms",
-        lax.all_gather(inv_diag, "cols", axis=2, tiled=True),
-        noise,
-        precision=precise,
-        preferred_element_type=jnp.float32,
+    driven = summed_around(
+        inv_diag,
+        "cols",
+        2,
+        lambda shard, offset: jnp.einsum(
+            "kmn,kns->kms",
+            shard,
+            lax.dynamic_slice_in_dim(noise, offset, shard.shape[2], axis=1),
+            precision=precise,
+            preferred_element_type=jnp.float32,
+        ),
     )
     local_field = driven[block_count - 1]
     reduced = coupling[block_count - 1]

time: 546 us -> 533 us (0.976)
  waiting for transfers between devices: 427 us -> 394 us
  matrix products: 57.1 us -> 68.4 us
  starting transfers between devices: 8.59 us -> 16.5 us
    ppermute x0 -> x3, waiting for transfers between devices: none -> 180 us  [summed_around(): carried = lax.ppermute(carried, axis, behind)]
    all_gather x1 -> x0, waiting for transfers between devices: 149 us -> none  [shards(): lax.all_gather(inv_diag, 'cols', axis=2, tiled=True)]
    all_gather x2, waiting for transfers between devices: 143 us -> 75.5 us  [shards(): lax.all_gather(coupling[block], 'cols', axis=1, tiled=True)]
    dot_general x1 -> x4, matrix products: 9.77 us -> 21 us  [shards(): jnp.einsum('kmn,kns->kms', shard, lax.dynamic_slice_in_dim(noise, offset,...]
    ppermute x0 -> x3, starting transfers between devices: none -> 8.15 us  [summed_around(): carried = lax.ppermute(carried, axis, behind)]
  transfers between devices with their start and end apart: 8 -> 10, of which waited for: 8 -> 9; matrix products, arithmetic and copies ran while one was open for 4% -> 6% of each run, Pallas kernels for 0% -> 0%
where the time goes in v1:
time: 533 us; the launch traced here: 532 us
  waiting for transfers between devices  394 us (74%)
  matrix products  68.4 us (13%)
  local copies, waits for them, and re-layouts  31 us (6%)
  starting transfers between devices  16.5 us (3%)
  between operations  13.3 us (2%)
  other arithmetic  8.33 us (2%)
    ppermute x3, waiting for transfers between devices, summed_around(): carried = lax.ppermute(carried, axis, behind)  180 us
    all_gather x1, waiting for transfers between devices, shards(): reduced_full = lax.all_gather(reduced, 'cols', axis=1, tiled=True)  80.8 us
    all_gather x2, waiting for transfers between devices, shards(): lax.all_gather(coupling[block], 'cols', axis=1, tiled=True)  75.5 us
    ppermute x4, waiting for transfers between devices, shifted(): return lax.ppermute(block, axis, route)  57.4 us
    dot_general x4, matrix products, relay_step(): jnp.dot(reduced_full, incoming, precision=precise, preferred_element_type...  27.6 us
    dot_general x4, matrix products, shards(): jnp.einsum('kmn,kns->kms', shard, lax.dynamic_slice_in_dim(noise, offset,...  21 us
    dot_general x3, matrix products, fold_with(): jnp.dot(segment, operand, precision=precise, preferred_element_type=jnp.f...  19.8 us
  transfers between devices with their start and end apart: 10, of which 9 were waited for; matrix products, arithmetic and copies ran while one was open for 6% of the time, Pallas kernels for 0%

profile of v1, /device:TPU:1, one launch (start us, length us, event | category | flops | bytes accessed | tf_op | source)
XLA Modules:
  0.0 532.0 jit_solution(11537229079705896311)
XLA Ops:
  6.5 0.0 copy-start
  6.5 0.0 all-gather.8.cloned.1.call-start
  6.5 4.2 collective-permute-start.1
  10.7 3.0 fusion.43
  13.7 0.0 all-gather.8.cloned.1.call-update
  13.7 0.0 all-gather.6.cloned.1.call-start
  13.8 101.2 %collective-permute-done.1 = f32[2,1024,256]{2,1,0:T(8,128)} collective-permute-done((f32[2,1024,256]{2,1,0:T(8,128)}, f32[2,1024,256]{2,1,0:T(8,128)}, u32[]{:S(2)}, u32[]{:S(2)}) %collective-permute-start.1) | collective-permute-done | bytes 2097184 | tf_op jit(solution)/shard_map/ppermute | solution.py:16
  115.0 0.0 collective-permute-start.2
  115.0 52.6 %collective-permute-done.2 = f32[2,1024,256]{2,1,0:T(8,128)} collective-permute-done((f32[2,1024,256]{2,1,0:T(8,128)}, f32[2,1024,256]{2,1,0:T(8,128)}, u32[]{:S(2)}, u32[]{:S(2)}) %collective-permute-start.2) | collective-permute-done | bytes 2097184 | tf_op jit(solution)/shard_map/ppermute | solution.py:16
  167.6 4.0 collective-permute-start.3
  171.6 1.6 copy.28
  173.1 0.0 copy-start.5
  173.2 0.0 copy-done
  173.2 5.4 %fusion.34 = f32[2,256,1024]{2,1,0:T(8,128)S(1)} fusion(f32[2,1024,256]{2,1,0:T(8,128)} %param.7, f32[2,1024,256]{2,1,0:T(8,128)S(1)} %copy-done, s32[]{:T(128)S(6)} %select_n.37), kind=kOutput, calls=%fused_computation.28 | convolution fusion | flops 1610612736 | bytes 4718596 | tf_op jit(solution)/shard_map/kmn,kns->kms/dot_general | solution.py:38
  178.6 5.1 fusion.32
  183.7 5.1 fusion.30
  188.8 26.2 %collective-permute-done.3 = f32[2,1024,256]{2,1,0:T(8,128)} collective-permute-done((f32[2,1024,256]{2,1,0:T(8,128)}, f32[2,1024,256]{2,1,0:T(8,128)}, u32[]{:S(2)}, u32[]{:S(2)}) %collective-permute-start.3) | collective-permute-done | bytes 2097184 | tf_op jit(solution)/shard_map/ppermute | solution.py:16
  215.0 5.4 %add_bitcast_fusion = f32[2,1024,256]{1,2,0:T(8,128)S(1)} fusion(f32[2,256,1024]{2,1,0:T(8,128)S(1)} %fusion.30, f32[2,256,1024]{2,1,0:T(8,128)S(1)} %fusion.34, f32[2,256,1024]{2,1,0:T(8,128)S(1)} %fusion.32, f32[2,1024,256]{2,1,0:T(8,128)} %collective-permute-done.3, f32[2,1024,256]{2,1,0:T(8,128)S(1)} %copy-done, s32[]{:T(128)S(6)} %select_n.43), kind=kOutput, calls=%fused_computation.13 | convolution fusion | flops 1612185600 | bytes 11010052 | tf_op jit(solution)/shard_map/kmn,kns->kms/dot_general | solution.py:38
  220.4 0.0 copy-start.1
  220.4 1.3 copy-done.1
  221.7 1.1 slice_bitcast_fusion
  222.8 0.0 all-gather.8.cloned.1.call-done
  222.8 0.0 copy-done.5
  222.8 0.0 copy-start.2
  222.8 9.5 %fusion.9 = f32[1024,512]{0,1:T(8,128)S(1)} fusion(f32[1,1024,1024]{2,1,0:T(8,128)} %all-gather.8.cloned.1.call-done, f32[1024,256]{0,1:T(8,128)S(1)} %bitcast.63, f32[1024,256]{0,1:T(8,128)} %slice_bitcast_fusion), kind=kOutput, calls=%fused_computation.14 | convolution fusion | flops 6442975232 | bytes 8388608 | tf_op jit(solution)/shard_map/dot_general | solution.py:28
  232.3 0.0 copy-done.2
  232.3 1.6 fusion.42
  233.9 0.0 copy-start.6
  233.9 0.0 all-gather.6.cloned.1.call-update
  233.9 0.0 all-gather.10.cloned.1.call-start
  234.0 0.7 all-gather.10.cloned.1.call-update
  234.7 0.0 copy-done.6
  234.7 1.6 copy.19
  236.3 1.0 copy.30
  237.3 80.8 %all-gather.6.cloned.1.call-done = f32[1024,1024]{0,1:T(8,128)} async-done(((f32[1024,256]{0,1:T(8,128)}), f32[1024,1024]{0,1:T(8,128)}) %all-gather.6.cloned.1.call-update) | async-done | bytes 4194320 | tf_op jit(solution)/shard_map/all_gather | solution.py:53
  318.1 5.4 %copy.20 = f32[1024,1024]{1,0:T(8,128)} copy(f32[1024,1024]{0,1:T(8,128)} %all-gather.6.cloned.1.call-done) | data formatting | bytes 8388608 | tf_op jit(solution)/shard_map/while | solution.py:63
  323.4 75.5 %all-gather.10.cloned.1.call-done = f32[1,1024,1024]{1,2,0:T(8,128)} async-done(((f32[1,1024,256]{1,2,0:T(8,128)}), f32[1,1024,1024]{1,2,0:T(8,128)}) %all-gather.10.cloned.1.call-update) | async-done | bytes 4194320 | tf_op jit(solution)/shard_map/all_gather | solution.py:69
  399.0 93.3 %while.12 = (s32[]{:T(128)}, f32[1024,256]{1,0:T(8,128)}, f32[1024,256]{1,0:T(8,128)}, f32[1024,1024]{1,0:T(8,128)}, f32[1024,256]{1,0:T(8,128)S(1)}, /*index=5*/s32[]{:T(128)}) while((s32[]{:T(128)}, f32[1024,256]{1,0:T(8,128)}, f32[1024,256]{1,0:T(8,128)}, f32[1024,1024]{1,0:T(8,128)}, f32[1024,256]{1,0:T(8,128)S(1)}, ...), condition=%wide.region_1.2_spmd, body=%wide.region_0.1_spmd.sunk | while | flops 3221487616 | bytes 11534445 | solution.py:63
  399.0 2.6 collective-permute-start
  401.5 13.9 %collective-permute-done = f32[1024,256]{1,0:T(8,128)} collective-permute-done((f32[1024,256]{1,0:T(8,128)}, f32[1024,256]{1,0:T(8,128)}, u32[]{:S(2)}, u32[]{:S(2)}) %collective-permute-start) | collective-permute-done | bytes 1048608 | tf_op jit(solution)/shard_map/while/body/eval_jaxpr/ppermute | solution.py:24
  415.4 6.9 %convolution_add_fusion.2 = f32[1024,256]{1,0:T(8,128)} fusion(f32[1024,256]{1,0:T(8,128)S(1)} %get-tuple-element.101, f32[1024,1024]{1,0:T(8,128)} %get-tuple-element.100, f32[1024,256]{1,0:T(8,128)} %collective-permute-done), kind=kOutput, calls=%fused_computation.1.clone.1 | convolution fusion | flops 3221487616 | bytes 7340032 | tf_op jit(solution)/shard_map/while/body/eval_jaxpr/dot_general | solution.py:58
  422.3 1.9 collective-permute-start
  424.2 14.5 %collective-permute-done = f32[1024,256]{1,0:T(8,128)} collective-permute-done((f32[1024,256]{1,0:T(8,128)}, f32[1024,256]{1,0:T(8,128)}, u32[]{:S(2)}, u32[]{:S(2)}) %collective-permute-start) | collective-permute-done | bytes 1048608 | tf_op jit(solution)/shard_map/while/body/eval_jaxpr/ppermute | solution.py:24
  438.8 6.9 %convolution_add_fusion.2 = f32[1024,256]{1,0:T(8,128)} fusion(f32[1024,256]{1,0:T(8,128)S(1)} %get-tuple-element.101, f32[1024,1024]{1,0:T(8,128)} %get-tuple-element.100, f32[1024,256]{1,0:T(8,128)} %collective-permute-done), kind=kOutput, calls=%fused_computation.1.clone.1 | convolution fusion | flops 3221487616 | bytes 7340032 | tf_op jit(solution)/shard_map/while/body/eval_jaxpr/dot_general | solution.py:58
  445.6 1.9 collective-permute-start
  447.6 14.5 %collective-permute-done = f32[1024,256]{1,0:T(8,128)} collective-permute-done((f32[1024,256]{1,0:T(8,128)}, f32[1024,256]{1,0:T(8,128)}, u32[]{:S(2)}, u32[]{:S(2)}) %collective-permute-start) | collective-permute-done | bytes 1048608 | tf_op jit(solution)/shard_map/while/body/eval_jaxpr/ppermute | solution.py:24
  462.1 6.9 %convolution_add_fusion.2 = f32[1024,256]{1,0:T(8,128)} fusion(f32[1024,256]{1,0:T(8,128)S(1)} %get-tuple-element.101, f32[1024,1024]{1,0:T(8,128)} %get-tuple-element.100, f32[1024,256]{1,0:T(8,128)} %collective-permute-done), kind=kOutput, calls=%fused_computation.1.clone.1 | convolution fusion | flops 3221487616 | bytes 7340032 | tf_op jit(solution)/shard_map/while/body/eval_jaxpr/dot_general | solution.py:58
  469.0 1.9 collective-permute-start
  470.9 14.5 %collective-permute-done = f32[1024,256]{1,0:T(8,128)} collective-permute-done((f32[1024,256]{1,0:T(8,128)}, f32[1024,256]{1,0:T(8,128)}, u32[]{:S(2)}, u32[]{:S(2)}) %collective-permute-start) | collective-permute-done | bytes 1048608 | tf_op jit(solution)/shard_map/while/body/eval_jaxpr/ppermute | solution.py:24
  485.4 6.9 %convolution_add_fusion.2 = f32[1024,256]{1,0:T(8,128)} fusion(f32[1024,256]{1,0:T(8,128)S(1)} %get-tuple-element.101, f32[1024,1024]{1,0:T(8,128)} %get-tuple-element.100, f32[1024,256]{1,0:T(8,128)} %collective-permute-done), kind=kOutput, calls=%fused_computation.1.clone.1 | convolution fusion | flops 3221487616 | bytes 7340032 | tf_op jit(solution)/shard_map/while/body/eval_jaxpr/dot_general | solution.py:58
  492.3 0.0 copy-start.3
  492.3 0.0 copy-start.4
  492.3 6.6 %fusion.26 = f32[1024,256]{0,1:T(8,128)S(1)} fusion(f32[1024,256]{1,0:T(8,128)} %get-tuple-element.31, f32[1,1024,1024]{1,2,0:T(8,128)} %all-gather.10.cloned.1.call-done, f32[2,1024,256]{1,2,0:T(8,128)} %copy-done.1), kind=kOutput, calls=%fused_computation.19 | convolution fusion | flops 3221487616 | bytes 7340032 | tf_op jit(solution)/shard_map/dot_general | solution.py:28
  498.8 0.0 copy-done.3
  498.9 0.0 copy-done.4
  498.9 3.7 fusion.20
  502.6 1.5 pad_maximum_fusion
  504.1 4.1 copy.22
  508.2 10.5 %gather_fusion = f32[1024,2,256]{2,1,0:T(2,128)} fusion(f32[2,1024,256]{2,0,1:T(2,128)} %copy.22, s32[1024]{0:T(1024)S(1)} %fusion.36), kind=kCustom, calls=%fused_computation | custom fusion | bytes 4198400 | tf_op jit(solution)/shard_map/jit(_take)/gather | solution.py:73
  518.7 5.2 select_bitcast_fusion
  523.9 1.5 copy.23
  (3 shorter events, 0.0 us)
Async XLA Ops:
  6.5 166.6 %copy-start = (f32[2,1024,256]{2,1,0:T(8,128)S(1)}, f32[2,1024,256]{2,1,0:T(8,128)}, u32[]{:S(2)}) copy-start(f32[2,1024,256]{2,1,0:T(8,128)} %param.6) | copy-start | bytes 6291460
  6.5 216.2 %all-gather.8.cloned.1.call-start = ((), (), s32[]{:S(2)}) async-start(), calls=%async_computation.1 | async-start | bytes 5242880 | tf_op jit(solution)/shard_map/all_gather | solution.py:69
  6.5 108.5 %collective-permute-start.1 = (f32[2,1024,256]{2,1,0:T(8,128)}, f32[2,1024,256]{2,1,0:T(8,128)}, u32[]{:S(2)}, u32[]{:S(2)}) collective-permute-start(f32[2,1024,256]{2,1,0:T(8,128)} %param.7), channel_id=1, source_target_pairs={{0,3},{1,0},{2,1},{3,2},{4,7},{5,4},{6,5},{7,6},{8,11},{9,8},{10,9... | collective-permute-start | bytes 6291464 | tf_op jit(solution)/shard_map/ppermute | solution.py:16
  13.7 304.4 %all-gather.6.cloned.1.call-start = ((), (), s32[]{:S(2)}) async-start(), calls=%async_computation | async-start | bytes 5242880 | tf_op jit(solution)/shard_map/all_gather | solution.py:53
  115.0 52.6 %collective-permute-start.2 = (f32[2,1024,256]{2,1,0:T(8,128)}, f32[2,1024,256]{2,1,0:T(8,128)}, u32[]{:S(2)}, u32[]{:S(2)}) collective-permute-start(f32[2,1024,256]{2,1,0:T(8,128)} %collective-permute-done.1), channel_id=1, source_target_pairs={{0,3},{1,0},{2,1},{3,2},{4,7},{5,4},{6,5},{7,6},{8,11},{9,8},{10,9... | collective-permute-start | bytes 6291464 | tf_op jit(solution)/shard_map/ppermute | solution.py:16
  167.6 47.4 %collective-permute-start.3 = (f32[2,1024,256]{2,1,0:T(8,128)}, f32[2,1024,256]{2,1,0:T(8,128)}, u32[]{:S(2)}, u32[]{:S(2)}) collective-permute-start(f32[2,1024,256]{2,1,0:T(8,128)} %collective-permute-done.2), channel_id=1, source_target_pairs={{0,3},{1,0},{2,1},{3,2},{4,7},{5,4},{6,5},{7,6},{8,11},{9,8},{10,9... | collective-permute-start | bytes 6291464 | tf_op jit(solution)/shard_map/ppermute | solution.py:16
  173.1 49.6 %copy-start.5 = (f32[1,1024,256]{1,2,0:T(8,128)}, f32[1,1024,256]{1,2,0:T(8,128)S(1)}, u32[]{:S(2)}) copy-start(f32[1,1024,256]{1,2,0:T(8,128)S(1)} %copy.28) | copy-start | bytes 3145732
  220.4 1.3 copy-start.1
  222.8 9.5 %copy-start.2 = (f32[2,1024,256]{1,2,0:T(8,128)S(1)}, f32[2,1024,256]{1,2,0:T(8,128)}, u32[]{:S(2)}) copy-start(f32[2,1024,256]{1,2,0:T(8,128)} %copy-done.1) | copy-start | bytes 6291460
  233.9 0.8 copy-start.6
  233.9 165.0 %all-gather.10.cloned.1.call-start = ((), (), s32[]{:S(2)}) async-start(), calls=%async_computation.2 | async-start | bytes 5242880 | tf_op jit(solution)/shard_map/all_gather | solution.py:69
  399.0 16.5 %collective-permute-start = (f32[1024,256]{1,0:T(8,128)}, f32[1024,256]{1,0:T(8,128)}, u32[]{:S(2)}, u32[]{:S(2)}) collective-permute-start(f32[1024,256]{1,0:T(8,128)} %get-tuple-element.92), channel_id=1, source_target_pairs={{4,0},{8,4},{12,8},{5,1},{9,5},{13,9},{6,2},{10,6},{14,10},{7,3},{... | collective-permute-start | bytes 3145736 | tf_op jit(solution)/shard_map/while/body/eval_jaxpr/ppermute | solution.py:24
  422.3 16.4 %collective-permute-start = (f32[1024,256]{1,0:T(8,128)}, f32[1024,256]{1,0:T(8,128)}, u32[]{:S(2)}, u32[]{:S(2)}) collective-permute-start(f32[1024,256]{1,0:T(8,128)} %get-tuple-element.92), channel_id=1, source_target_pairs={{4,0},{8,4},{12,8},{5,1},{9,5},{13,9},{6,2},{10,6},{14,10},{7,3},{... | collective-permute-start | bytes 3145736 | tf_op jit(solution)/shard_map/while/body/eval_jaxpr/ppermute | solution.py:24
  445.6 16.4 %collective-permute-start = (f32[1024,256]{1,0:T(8,128)}, f32[1024,256]{1,0:T(8,128)}, u32[]{:S(2)}, u32[]{:S(2)}) collective-permute-start(f32[1024,256]{1,0:T(8,128)} %get-tuple-element.92), channel_id=1, source_target_pairs={{4,0},{8,4},{12,8},{5,1},{9,5},{13,9},{6,2},{10,6},{14,10},{7,3},{... | collective-permute-start | bytes 3145736 | tf_op jit(solution)/shard_map/while/body/eval_jaxpr/ppermute | solution.py:24
  469.0 16.4 %collective-permute-start = (f32[1024,256]{1,0:T(8,128)}, f32[1024,256]{1,0:T(8,128)}, u32[]{:S(2)}, u32[]{:S(2)}) collective-permute-start(f32[1024,256]{1,0:T(8,128)} %get-tuple-element.92), channel_id=1, source_target_pairs={{4,0},{8,4},{12,8},{5,1},{9,5},{13,9},{6,2},{10,6},{14,10},{7,3},{... | collective-permute-start | bytes 3145736 | tf_op jit(solution)/shard_map/while/body/eval_jaxpr/ppermute | solution.py:24
  492.3 6.6 %copy-start.3 = (f32[2,1024,256]{1,2,0:T(8,128)S(1)}, f32[2,1024,256]{1,2,0:T(8,128)}, u32[]{:S(2)}) copy-start(f32[2,1024,256]{1,2,0:T(8,128)} %copy-done.1) | copy-start | bytes 6291460
  492.3 6.6 %copy-start.4 = (f32[1,1024,1024]{2,1,0:T(8,128)S(1)}, f32[1,1024,1024]{2,1,0:T(8,128)}, u32[]{:S(2)}) copy-start(f32[1,1024,1024]{2,1,0:T(8,128)} %all-gather.8.cloned.1.call-done) | copy-start | bytes 12582916
Sparse Core Ops, SparseCore 0:
  13.8 117.0 all-gather.7
  234.1 83.9 all-gather.5
  319.6 79.2 all-gather.9
